TPU v7x, 512 devices: a whole 4x4x16 slice. The times are simulated.
512 devices in a mesh: gx: 64 (over z, y), gy: 8 (over x, core).
Axes of the slice: x: 4, y: 4, z: 16, core: 2. Of those that a mesh axis runs over, the one named last changes fastest.
Arguments:
- rhs: float32 [64, 8, 128, 128], P('gx', 'gy'), may hold values from -57 to 57
- face_rows: int32 [64, 8, 4, 128], P('gx', 'gy'), may hold values from 0 to 127
- margin_weight: float32 [64, 8, 4, 128], P('gx', 'gy'), may hold values from 0.2 to 1
- local_blocks: bfloat16 [64, 8, 1, 128, 128], P('gx', 'gy'), may hold values from -0.4 to 4.4
- subdomain_inverse: bfloat16 [64, 8, 128, 640], P('gx', 'gy'), may hold values from -0.4 to 1.8
- coarse_basis: bfloat16 [64, 8, 128, 32], P('gx', 'gy'), may hold values from -0.5 to 0.5
- coarse_inverse: bfloat16 [64, 8, 32, 16384], P('gx', 'gy'), may hold values from -0.09765625 to 0.09765625
- coarse_map: int32 [512], replicated, may hold values from 0 to 511, each once
Outputs:
- solution: float32 [64, 8, 128, 128], P('gx', 'gy')
- relative_residual: float32 [128], replicated
Inputs may be any that keep to these rules, and one draw needn't show every extreme that they name: `face_rows`: rows of the subdomain, repeats possible. `coarse_map`: every position once.
All inputs are finite; a program needn't handle non-finite values.
Results may differ from a plain program's by a relative error of at most 0.004.
Values may be sent and summed in bfloat16 or wider, within the bound.
No kernel may reach another device: no remote copies, remote signals or barrier semaphores. Data moves between devices by JAX's collectives and lax.ppermute only.
A program may use at most 64 MiB of HBM per device.

v0:
```python
import jax
import jax.numpy as jnp
from jax import lax
from jax.sharding import PartitionSpec as P

EPSILON = 1e-06


def neighbours(rows, axis):
    count = lax.axis_size(axis)
    up = [(i, i + 1) for i in range(count - 1)]
    down = [(i + 1, i) for i in range(count - 1)]
    return (lax.ppermute(rows[1], axis, up), lax.ppermute(rows[0], axis, down))


def exchange(packs):
    below_first, above_first = neighbours(packs[0:2], "gx")
    below_second, above_second = neighbours(packs[2:4], "gy")
    return jnp.stack([below_first, above_first, below_second, above_second], axis=0)


def allsum(value):
    for axis in ("gy", "gx"):
        count = lax.axis_size(axis)
        if count & count - 1:
            value = lax.psum(value, axis)
            continue
        step = 1
        while step < count:
            value = value + lax.ppermute(value, axis, [(i, i ^ step) for i in range(count)])
            step *= 2
    return value


def least_squares(scale_norm, first_dot, first_norm, cross_dot, second_dot, second_norm):
    radius_one = jnp.sqrt(first_dot * first_dot + first_norm * first_norm)
    cosine_one = first_dot / radius_one
    sine_one = first_norm / radius_one
    upper_entry = cosine_one * cross_dot + sine_one * second_dot
    lower_entry = cosine_one * second_dot - sine_one * cross_dot
    radius_two = jnp.sqrt(lower_entry * lower_entry + second_norm * second_norm)
    cosine_two = lower_entry / radius_two
    sine_two = second_norm / radius_two
    weight_two = -cosine_two * sine_one * scale_norm / radius_two
    weight_one = (cosine_one * scale_norm - upper_entry * weight_two) / radius_one
    return (weight_one, weight_two, sine_one * sine_two)


def on_device(
    rhs,
    face_rows,
    margin_weight,
    local_blocks,
    subdomain_inverse,
    coarse_basis,
    coarse_inverse,
    coarse_map,
):
    right_side = rhs[0, 0]
    margin_rows = face_rows[0, 0]
    margin_weights = margin_weight[0, 0]
    local_block = local_blocks[0, 0]
    inverse_rows = subdomain_inverse[0, 0]
    basis = coarse_basis[0, 0]
    coarse_rows = coarse_inverse[0, 0]
    owned_rows = right_side.shape[0]
    system_count = right_side.shape[1]
    basis_count = basis.shape[1]
    block_rows = local_block.shape[1]
    count_x = lax.axis_size("gx")
    count_y = lax.axis_size("gy")
    gathered_map = coarse_map.reshape(count_x, count_y).T.reshape(-1)
    positions = (
        gathered_map[:, None] * basis_count + jnp.arange(basis_count, dtype=jnp.int32)[None, :]
    ).reshape(-1)
    permuted = jnp.take(coarse_rows, positions, axis=1)

    def margin_of(field):
        return exchange(field[margin_rows])

    def coarse_gather(residual):
        return lax.all_gather(
            lax.all_gather(residual, "gx", axis=0, tiled=True), "gy", axis=0, tiled=True
        )

    def precondition(rounded, margin):
        extended = jnp.concatenate([rounded, margin.reshape(-1, system_count)], axis=0)
        local_part = jnp.dot(inverse_rows, extended, preferred_element_type=jnp.float32)
        residual = lax.dot_general(
            basis, rounded, (((0,), (0,)), ((), ())), preferred_element_type=jnp.float32
        ).astype(jnp.bfloat16)
        solved = jnp.dot(permuted, coarse_gather(residual), preferred_element_type=jnp.float32)
        return local_part + jnp.dot(
            basis, solved.astype(jnp.bfloat16), preferred_element_type=jnp.float32
        )

    def apply_operator(vector):
        rounded = vector.astype(jnp.bfloat16)
        own_part = jnp.einsum(
            "brc,bcn->brn",
            local_block,
            rounded.reshape(-1, block_rows, system_count),
            preferred_element_type=jnp.float32,
        ).reshape(owned_rows, system_count)
        weighted = margin_weights[:, :, None] * margin_of(rounded).astype(jnp.float32)
        coupling = (
            jnp.zeros((owned_rows, system_count), jnp.float32)
            .at[margin_rows.reshape(-1)]
            .add(weighted.reshape(-1, system_count))
        )
        return own_part - coupling

    def column_norm(vector):
        return jnp.sqrt(allsum(jnp.sum(vector * vector, axis=0)) + EPSILON)

    rhs_margin = margin_of(right_side)
    scale_norm = column_norm(right_side)
    krylov_one = right_side / scale_norm
    margin_one = rhs_margin / scale_norm
    precond_one = precondition(krylov_one.astype(jnp.bfloat16), margin_one.astype(jnp.bfloat16))
    applied = apply_operator(precond_one)
    applied_margin = margin_of(applied)
    first_dot = allsum(jnp.sum(applied * krylov_one, axis=0))
    remainder = applied - first_dot * krylov_one
    first_norm = column_norm(remainder)
    krylov_two = remainder / first_norm
    margin_two = (applied_margin - first_dot * margin_one) / first_norm
    precond_two = precondition(krylov_two.astype(jnp.bfloat16), margin_two.astype(jnp.bfloat16))
    applied = apply_operator(precond_two)
    dots = allsum(
        jnp.stack([jnp.sum(applied * krylov_one, axis=0), jnp.sum(applied * krylov_two, axis=0)])
    )
    cross_dot = dots[0]
    second_dot = dots[1]
    remainder = applied - cross_dot * krylov_one - second_dot * krylov_two
    second_norm = column_norm(remainder)
    weight_one, weight_two, relative = least_squares(
        scale_norm, first_dot, first_norm, cross_dot, second_dot, second_norm
    )
    solution = weight_one * precond_one + weight_two * precond_two
    return (solution[None, None], relative)


def solution(mesh):
    return jax.shard_map(
        on_device,
        mesh=mesh,
        in_specs=(
            P("gx", "gy", None, None),
            P("gx", "gy", None, None),
            P("gx", "gy", None, None),
            P("gx", "gy", None, None, None),
            P("gx", "gy", None, None),
            P("gx", "gy", None, None),
            P("gx", "gy", None, None),
            P(),
        ),
        out_specs=(P("gx", "gy", None, None), P()),
        check_vma=False,
    )
```

profile of v0, /device:TPU:2, one launch (start us, length us, event | category | flops | bytes accessed | tf_op | source)
XLA Modules:
  0.0 728.0 jit_solution(14645991461228601917)
XLA Ops:
  11.3 7.8 %collective-permute-start.1 = (f32[128]{0:T(128)S(1)}, f32[128]{0:T(128)S(1)}, u32[]{:S(2)}, u32[]{:S(2)}) collective-permute-start(f32[128]{0:T(128)S(1)} %add.245), channel_id=1, source_target_pairs={{0,2},{1,3},{2,0},{3,1},{4,6},{5,7},{6,4},{7,5},{8,10},{9,11},{10,... | collective-permute-start | bytes 1544 | tf_op jit(solution)/shard_map/ppermute | solution.py:30
  22.5 5.0 collective-permute-done.2
  34.9 5.0 collective-permute-done.4
  51.8 5.6 collective-permute-start.7
  61.1 11.8 %collective-permute-start.8 = (f32[128]{0:T(128)S(1)}, f32[128]{0:T(128)S(1)}, u32[]{:S(2)}, u32[]{:S(2)}) collective-permute-start(f32[128]{0:T(128)S(1)} %add.252), channel_id=1, source_target_pairs={{0,256},{8,264},{16,272},{24,280},{32,288},{40,296},{48,304},{56,3... | collective-permute-start | bytes 1544 | tf_op jit(solution)/shard_map/ppermute | solution.py:30
  76.3 111.9 %all_gather.12 = bf16[2048,128]{1,0:T(8,128)(2,1)} all-gather(bf16[32,128]{1,0:T(8,128)(2,1)S(1)} %fusion.6), channel_id=1, replica_groups=mesh['gx'=64,'gy'=8] {'gx'}, dimensions={0}, use_global_device_ids=true | all-gather | bytes 532480 | tf_op jit(solution)/shard_map/all_gather | solution.py:83
  204.4 58.2 %gather_fusion.1 = bf16[16384,32]{1,0:T(8,128)(2,1)} fusion(bf16[32,16384]{0,1:T(8,128)(2,1)} %bitcast.133, s32[16384]{0:T(1024)S(1)} %broadcast_clamp_fusion), kind=kCustom, calls=%fused_computation.1 | custom fusion | bytes 2162688 | tf_op jit(solution)/shard_map/jit(_take)/gather | solution.py:76
  263.1 7.1 convolution_add_fusion.1
  309.6 6.4 collective-permute-start.21
  317.5 7.1 collective-permute-start.22
  332.5 8.3 %collective-permute-start.24 = (f32[128]{0:T(128)S(1)}, f32[128]{0:T(128)S(1)}, u32[]{:S(2)}, u32[]{:S(2)}) collective-permute-start(f32[128]{0:T(128)S(1)} %add.273), channel_id=1, source_target_pairs={{0,128},{8,136},{16,144},{24,152},{32,160},{40,168},{48,176},{56,1... | collective-permute-start | bytes 1544 | tf_op jit(solution)/shard_map/ppermute | solution.py:30
  342.4 11.4 %collective-permute-start.25 = (f32[128]{0:T(128)S(1)}, f32[128]{0:T(128)S(1)}, u32[]{:S(2)}, u32[]{:S(2)}) collective-permute-start(f32[128]{0:T(128)S(1)} %add.274), channel_id=1, source_target_pairs={{0,256},{8,264},{16,272},{24,280},{32,288},{40,296},{48,304},{56,3... | collective-permute-start | bytes 1544 | tf_op jit(solution)/shard_map/ppermute | solution.py:30
  396.3 7.8 %collective-permute-start.33 = (f32[128]{0:T(128)S(1)}, f32[128]{0:T(128)S(1)}, u32[]{:S(2)}, u32[]{:S(2)}) collective-permute-start(f32[128]{0:T(128)S(1)} %add.282), channel_id=1, source_target_pairs={{0,128},{8,136},{16,144},{24,152},{32,160},{40,168},{48,176},{56,1... | collective-permute-start | bytes 1544 | tf_op jit(solution)/shard_map/ppermute | solution.py:30
  405.7 11.4 %collective-permute-start.34 = (f32[128]{0:T(128)S(1)}, f32[128]{0:T(128)S(1)}, u32[]{:S(2)}, u32[]{:S(2)}) collective-permute-start(f32[128]{0:T(128)S(1)} %add.283), channel_id=1, source_target_pairs={{0,256},{8,264},{16,272},{24,280},{32,288},{40,296},{48,304},{56,3... | collective-permute-start | bytes 1544 | tf_op jit(solution)/shard_map/ppermute | solution.py:30
  420.0 108.2 %all_gather.14 = bf16[2048,128]{1,0:T(8,128)(2,1)} all-gather(bf16[32,128]{1,0:T(8,128)(2,1)S(1)} %fusion.7), channel_id=1, replica_groups=mesh['gx'=64,'gy'=8] {'gx'}, dimensions={0}, use_global_device_ids=true | all-gather | bytes 532480 | tf_op jit(solution)/shard_map/all_gather | solution.py:83
  542.1 22.8 %all-gather.5.cloned.1.call-done = bf16[16384,128]{1,0:T(8,128)(2,1)} async-done(((bf16[2048,128]{1,0:T(8,128)(2,1)}), bf16[16384,128]{1,0:T(8,128)(2,1)}) %all-gather.5.cloned.1.call-update) | async-done | bytes 4194320 | tf_op jit(solution)/shard_map/all_gather | solution.py:82
  564.8 7.1 convolution_add_fusion
  610.1 5.4 collective-permute-start.47
  617.1 6.1 collective-permute-start.48
  631.2 9.2 %collective-permute-start.50 = (f32[2,128]{1,0:T(2,128)S(1)}, f32[2,128]{1,0:T(2,128)S(1)}, u32[]{:S(2)}, u32[]{:S(2)}) collective-permute-start(f32[2,128]{1,0:T(2,128)S(1)} %add.294), channel_id=1, source_target_pairs={{0,128},{8,136},{16,144},{24,152},{32,160},{40,168},{48,176},{56,1... | collective-permute-start | bytes 3080 | tf_op jit(solution)/shard_map/ppermute | solution.py:30
  641.9 13.0 %collective-permute-start.51 = (f32[2,128]{1,0:T(2,128)S(1)}, f32[2,128]{1,0:T(2,128)S(1)}, u32[]{:S(2)}, u32[]{:S(2)}) collective-permute-start(f32[2,128]{1,0:T(2,128)S(1)} %add.295), channel_id=1, source_target_pairs={{0,256},{8,264},{16,272},{24,280},{32,288},{40,296},{48,304},{56,3... | collective-permute-start | bytes 3080 | tf_op jit(solution)/shard_map/ppermute | solution.py:30
  679.4 5.0 collective-permute-done.56
  696.2 7.5 %collective-permute-start.59 = (f32[128]{0:T(128)S(1)}, f32[128]{0:T(128)S(1)}, u32[]{:S(2)}, u32[]{:S(2)}) collective-permute-start(f32[128]{0:T(128)S(1)} %add.304), channel_id=1, source_target_pairs={{0,128},{8,136},{16,144},{24,152},{32,160},{40,168},{48,176},{56,1... | collective-permute-start | bytes 1544 | tf_op jit(solution)/shard_map/ppermute | solution.py:30
  705.6 12.6 %collective-permute-start.60 = (f32[128]{0:T(128)S(1)}, f32[128]{0:T(128)S(1)}, u32[]{:S(2)}, u32[]{:S(2)}) collective-permute-start(f32[128]{0:T(128)S(1)} %add.305), channel_id=1, source_target_pairs={{0,256},{8,264},{16,272},{24,280},{32,288},{40,296},{48,304},{56,3... | collective-permute-start | bytes 1544 | tf_op jit(solution)/shard_map/ppermute | solution.py:30
  (220 shorter events, 251.2 us)
Async XLA Ops:
  7.2 255.8 %all-gather.3.cloned.1.call-start = ((), (), s32[]{:S(2)}) async-start(), calls=%async_computation | async-start | bytes 4718592 | tf_op jit(solution)/shard_map/all_gather | solution.py:82
  11.3 9.3 %collective-permute-start.1 = (f32[128]{0:T(128)S(1)}, f32[128]{0:T(128)S(1)}, u32[]{:S(2)}, u32[]{:S(2)}) collective-permute-start(f32[128]{0:T(128)S(1)} %add.245), channel_id=1, source_target_pairs={{0,2},{1,3},{2,0},{3,1},{4,6},{5,7},{6,4},{7,5},{8,10},{9,11},{10,... | collective-permute-start | bytes 1544 | tf_op jit(solution)/shard_map/ppermute | solution.py:30
  51.8 9.4 %collective-permute-start.7 = (f32[128]{0:T(128)S(1)}, f32[128]{0:T(128)S(1)}, u32[]{:S(2)}, u32[]{:S(2)}) collective-permute-start(f32[128]{0:T(128)S(1)} %add.251), channel_id=1, source_target_pairs={{0,128},{8,136},{16,144},{24,152},{32,160},{40,168},{48,176},{56,1... | collective-permute-start | bytes 1544 | tf_op jit(solution)/shard_map/ppermute | solution.py:30
  61.1 14.2 %collective-permute-start.8 = (f32[128]{0:T(128)S(1)}, f32[128]{0:T(128)S(1)}, u32[]{:S(2)}, u32[]{:S(2)}) collective-permute-start(f32[128]{0:T(128)S(1)} %add.252), channel_id=1, source_target_pairs={{0,256},{8,264},{16,272},{24,280},{32,288},{40,296},{48,304},{56,3... | collective-permute-start | bytes 1544 | tf_op jit(solution)/shard_map/ppermute | solution.py:30
  188.2 376.6 %all-gather.5.cloned.1.call-start = ((), (), s32[]{:S(2)}) async-start(), calls=%async_computation.1 | async-start | bytes 4718592 | tf_op jit(solution)/shard_map/all_gather | solution.py:82
  190.9 71.8 %collective-permute-start.9 = (f32[128,128]{1,0:T(8,128)S(1)}, f32[128,128]{1,0:T(8,128)S(1)}, u32[]{:S(2)}, u32[]{:S(2)}) collective-permute-start(f32[128,128]{1,0:T(8,128)S(1)} %get-tuple-element.19), channel_id=1, source_target_pairs={{0,8},{8,16},{16,24},{24,32},{32,40},{40,48},{48,56},{56,64},{64,7... | collective-permute-start | bytes 196616 | tf_op jit(solution)/shard_map/ppermute | solution.py:13
  193.5 69.1 %collective-permute-start.11 = (f32[128,128]{1,0:T(8,128)S(1)}, f32[128,128]{1,0:T(8,128)S(1)}, u32[]{:S(2)}, u32[]{:S(2)}) collective-permute-start(f32[128,128]{1,0:T(8,128)S(1)} %get-tuple-element.20), channel_id=1, source_target_pairs={{0,1},{1,2},{2,3},{3,4},{4,5},{5,6},{6,7},{8,9},{9,10},{10,11},{11... | collective-permute-start | bytes 196616 | tf_op jit(solution)/shard_map/ppermute | solution.py:13
  195.4 67.2 %collective-permute-start.10 = (f32[128,128]{1,0:T(8,128)S(1)}, f32[128,128]{1,0:T(8,128)S(1)}, u32[]{:S(2)}, u32[]{:S(2)}) collective-permute-start(f32[128,128]{1,0:T(8,128)S(1)} %get-tuple-element.21), channel_id=1, source_target_pairs={{8,0},{16,8},{24,16},{32,24},{40,32},{48,40},{56,48},{64,56},{72,6... | collective-permute-start | bytes 196616 | tf_op jit(solution)/shard_map/ppermute | solution.py:13
  196.7 65.9 %collective-permute-start.12 = (f32[128,128]{1,0:T(8,128)S(1)}, f32[128,128]{1,0:T(8,128)S(1)}, u32[]{:S(2)}, u32[]{:S(2)}) collective-permute-start(f32[128,128]{1,0:T(8,128)S(1)} %get-tuple-element.22), channel_id=1, source_target_pairs={{1,0},{2,1},{3,2},{4,3},{5,4},{6,5},{7,6},{9,8},{10,9},{11,10},{12... | collective-permute-start | bytes 196616 | tf_op jit(solution)/shard_map/ppermute | solution.py:13
  271.6 11.2 %collective-permute-start.13 = (bf16[128,128]{1,0:T(8,128)(2,1)S(1)}, bf16[128,128]{1,0:T(8,128)(2,1)S(1)}, u32[]{:S(2)}, u32[]{:S(2)}) collective-permute-start(bf16[128,128]{1,0:T(8,128)(2,1)S(1)} %get-tuple-element.27), channel_id=1, source_target_pairs={{0,8},{8,16},{16,24},{24,32},{32,40},{40,48},{48,56},{56,64},{64,7... | collective-permute-start | bytes 98312 | tf_op jit(solution)/shard_map/ppermute | solution.py:13
  309.6 7.9 %collective-permute-start.21 = (f32[128]{0:T(128)S(1)}, f32[128]{0:T(128)S(1)}, u32[]{:S(2)}, u32[]{:S(2)}) collective-permute-start(f32[128]{0:T(128)S(1)} %add.270), channel_id=1, source_target_pairs={{0,16},{8,24},{16,0},{24,8},{32,48},{40,56},{48,32},{56,40},{64,80... | collective-permute-start | bytes 1544 | tf_op jit(solution)/shard_map/ppermute | solution.py:30
  317.5 8.7 %collective-permute-start.22 = (f32[128]{0:T(128)S(1)}, f32[128]{0:T(128)S(1)}, u32[]{:S(2)}, u32[]{:S(2)}) collective-permute-start(f32[128]{0:T(128)S(1)} %add.271), channel_id=1, source_target_pairs={{0,32},{8,40},{16,48},{24,56},{32,0},{40,8},{48,16},{56,24},{64,96... | collective-permute-start | bytes 1544 | tf_op jit(solution)/shard_map/ppermute | solution.py:30
  332.5 9.9 %collective-permute-start.24 = (f32[128]{0:T(128)S(1)}, f32[128]{0:T(128)S(1)}, u32[]{:S(2)}, u32[]{:S(2)}) collective-permute-start(f32[128]{0:T(128)S(1)} %add.273), channel_id=1, source_target_pairs={{0,128},{8,136},{16,144},{24,152},{32,160},{40,168},{48,176},{56,1... | collective-permute-start | bytes 1544 | tf_op jit(solution)/shard_map/ppermute | solution.py:30
  342.4 14.2 %collective-permute-start.25 = (f32[128]{0:T(128)S(1)}, f32[128]{0:T(128)S(1)}, u32[]{:S(2)}, u32[]{:S(2)}) collective-permute-start(f32[128]{0:T(128)S(1)} %add.274), channel_id=1, source_target_pairs={{0,256},{8,264},{16,272},{24,280},{32,288},{40,296},{48,304},{56,3... | collective-permute-start | bytes 1544 | tf_op jit(solution)/shard_map/ppermute | solution.py:30
  396.3 9.4 %collective-permute-start.33 = (f32[128]{0:T(128)S(1)}, f32[128]{0:T(128)S(1)}, u32[]{:S(2)}, u32[]{:S(2)}) collective-permute-start(f32[128]{0:T(128)S(1)} %add.282), channel_id=1, source_target_pairs={{0,128},{8,136},{16,144},{24,152},{32,160},{40,168},{48,176},{56,1... | collective-permute-start | bytes 1544 | tf_op jit(solution)/shard_map/ppermute | solution.py:30
  405.7 14.2 %collective-permute-start.34 = (f32[128]{0:T(128)S(1)}, f32[128]{0:T(128)S(1)}, u32[]{:S(2)}, u32[]{:S(2)}) collective-permute-start(f32[128]{0:T(128)S(1)} %add.283), channel_id=1, source_target_pairs={{0,256},{8,264},{16,272},{24,280},{32,288},{40,296},{48,304},{56,3... | collective-permute-start | bytes 1544 | tf_op jit(solution)/shard_map/ppermute | solution.py:30
  529.3 10.5 %collective-permute-start.35 = (f32[128,128]{1,0:T(8,128)S(1)}, f32[128,128]{1,0:T(8,128)S(1)}, u32[]{:S(2)}, u32[]{:S(2)}) collective-permute-start(f32[128,128]{1,0:T(8,128)S(1)} %get-tuple-element.15), channel_id=1, source_target_pairs={{0,8},{8,16},{16,24},{24,32},{32,40},{40,48},{48,56},{56,64},{64,7... | collective-permute-start | bytes 196616 | tf_op jit(solution)/shard_map/ppermute | solution.py:13
  532.8 7.1 collective-permute-start.37
  573.4 10.3 %collective-permute-start.39 = (bf16[128,128]{1,0:T(8,128)(2,1)S(1)}, bf16[128,128]{1,0:T(8,128)(2,1)S(1)}, u32[]{:S(2)}, u32[]{:S(2)}) collective-permute-start(bf16[128,128]{1,0:T(8,128)(2,1)S(1)} %get-tuple-element.23), channel_id=1, source_target_pairs={{0,8},{8,16},{16,24},{24,32},{32,40},{40,48},{48,56},{56,64},{64,7... | collective-permute-start | bytes 98312 | tf_op jit(solution)/shard_map/ppermute | solution.py:13
  617.1 7.6 %collective-permute-start.48 = (f32[2,128]{1,0:T(2,128)S(1)}, f32[2,128]{1,0:T(2,128)S(1)}, u32[]{:S(2)}, u32[]{:S(2)}) collective-permute-start(f32[2,128]{1,0:T(2,128)S(1)} %add.292), channel_id=1, source_target_pairs={{0,32},{8,40},{16,48},{24,56},{32,0},{40,8},{48,16},{56,24},{64,96... | collective-permute-start | bytes 3080 | tf_op jit(solution)/shard_map/ppermute | solution.py:30
  631.2 10.8 %collective-permute-start.50 = (f32[2,128]{1,0:T(2,128)S(1)}, f32[2,128]{1,0:T(2,128)S(1)}, u32[]{:S(2)}, u32[]{:S(2)}) collective-permute-start(f32[2,128]{1,0:T(2,128)S(1)} %add.294), channel_id=1, source_target_pairs={{0,128},{8,136},{16,144},{24,152},{32,160},{40,168},{48,176},{56,1... | collective-permute-start | bytes 3080 | tf_op jit(solution)/shard_map/ppermute | solution.py:30
  641.9 14.5 %collective-permute-start.51 = (f32[2,128]{1,0:T(2,128)S(1)}, f32[2,128]{1,0:T(2,128)S(1)}, u32[]{:S(2)}, u32[]{:S(2)}) collective-permute-start(f32[2,128]{1,0:T(2,128)S(1)} %add.295), channel_id=1, source_target_pairs={{0,256},{8,264},{16,272},{24,280},{32,288},{40,296},{48,304},{56,3... | collective-permute-start | bytes 3080 | tf_op jit(solution)/shard_map/ppermute | solution.py:30
  696.2 9.4 %collective-permute-start.59 = (f32[128]{0:T(128)S(1)}, f32[128]{0:T(128)S(1)}, u32[]{:S(2)}, u32[]{:S(2)}) collective-permute-start(f32[128]{0:T(128)S(1)} %add.304), channel_id=1, source_target_pairs={{0,128},{8,136},{16,144},{24,152},{32,160},{40,168},{48,176},{56,1... | collective-permute-start | bytes 1544 | tf_op jit(solution)/shard_map/ppermute | solution.py:30
  705.6 14.2 %collective-permute-start.60 = (f32[128]{0:T(128)S(1)}, f32[128]{0:T(128)S(1)}, u32[]{:S(2)}, u32[]{:S(2)}) collective-permute-start(f32[128]{0:T(128)S(1)} %add.305), channel_id=1, source_target_pairs={{0,256},{8,264},{16,272},{24,280},{32,288},{40,296},{48,304},{56,3... | collective-permute-start | bytes 1544 | tf_op jit(solution)/shard_map/ppermute | solution.py:30
  (47 other events, 1050.9 us)
Sparse Core Ops, SparseCore 0:
  188.4 33.9 all-gather.2
  528.4 36.4 all-gather.4
where the time goes:
time: 730 us; the launch traced here: 728 us
  starting transfers between devices  252 us (35%)
  blocking collectives  220 us (30%)
  waiting for transfers between devices  149 us (20%)
  local copies, waits for them, and re-layouts  68.5 us (9%)
  matrix products  16.1 us (2%)
  between operations  15 us (2%)
  other arithmetic  7.87 us (1%)
    all_gather x2, blocking collectives, coarse_gather(): lax.all_gather(residual, 'gx', axis=0, tiled=True)  220 us
    ppermute x45, starting transfers between devices, allsum(): lax.ppermute(value, axis, [(i, i ^ step) for i in range(count)])  210 us
    ppermute x45, waiting for transfers between devices, allsum(): lax.ppermute(value, axis, [(i, i ^ step) for i in range(count)])  121 us
    gather x1, local copies, waits for them, and re-layouts, on_device(): permuted = jnp.take(coarse_rows, positions, axis=1)  58.2 us
    ppermute x16, starting transfers between devices, neighbours(): return (lax.ppermute(rows[1], axis, up), lax.ppermute(rows[0], axis, down))  41.4 us
    all_gather x2, waiting for transfers between devices, coarse_gather(): lax.all_gather(lax.all_gather(residual, 'gx', axis=0, tiled=True), 'gy',...  22.8 us
  transfers between devices with their start and end apart: 63, of which 52 were waited for; matrix products, arithmetic and copies ran while one was open for 9% of the time, Pallas kernels for 0%

commit v1 on v0

--- a/solution.py
+++ b/solution.py
@@ -4,6 +4,33 @@
 from jax.sharding import PartitionSpec as P
 
 EPSILON = 1e-06
+
+
+def _test_ends(z_in, chip_axis):
+    raw_out, w_next, val2 = (
+        lax.psum(1, axis_name=chip_axis),
+        lax.axis_index(chip_axis),
+        z_in.shape[0],
+    )
+    line_up = []
+    for num in range(raw_out):
+        line_up.append((num, (num + 1) % raw_out))
+    by_place = []
+    for num in range(raw_out):
+        by_place.append((num, (num - 1) % raw_out))
+    z1 = jnp.zeros((*z_in.shape[:0], raw_out * val2, *z_in.shape[1:]), z_in.dtype)
+    z1 = lax.dynamic_update_slice_in_dim(z1, z_in, w_next * val2, axis=0)
+    w2 = reached = z_in
+    taken_in = raw_out // 2
+    for kk in range(1, taken_in + 1):
+        w2 = lax.ppermute(w2, axis_name=chip_axis, perm=line_up)
+        z1 = lax.dynamic_update_slice_in_dim(z1, w2, (w_next - kk) % raw_out * val2, axis=0)
+        if kk < raw_out - taken_in:
+            reached = lax.ppermute(reached, axis_name=chip_axis, perm=by_place)
+            z1 = lax.dynamic_update_slice_in_dim(
+                z1, reached, (w_next + kk) % raw_out * val2, axis=0
+            )
+    return z1
 
 
 def neighbours(rows, axis):
@@ -79,9 +106,7 @@
         return exchange(field[margin_rows])
 
     def coarse_gather(residual):
-        return lax.all_gather(
-            lax.all_gather(residual, "gx", axis=0, tiled=True), "gy", axis=0, tiled=True
-        )
+        return _test_ends(lax.all_gather(residual, "gx", axis=0, tiled=True), "gy")
 
     def precondition(rounded, margin):
         extended = jnp.concatenate([rounded, margin.reshape(-1, system_count)], axis=0)

time: 730 us -> 735 us (level)
  the two profiles are of different devices: /device:TPU:2 before, /device:TPU:32 now
where the time goes in v1:
time: 735 us; the launch traced here: 733 us
  starting transfers between devices  219 us (30%)
  blocking collectives  202 us (27%)
  waiting for transfers between devices  201 us (27%)
  local copies, waits for them, and re-layouts  86 us (12%)
  matrix products  15.2 us (2%)
  other arithmetic  8.54 us (1%)
    all_gather x2, blocking collectives, coarse_gather(): return _test_ends(lax.all_gather(residual, 'gx', axis=0, tiled=True), 'gy')  202 us
    ppermute x45, starting transfers between devices, allsum(): lax.ppermute(value, axis, [(i, i ^ step) for i in range(count)])  155 us
    ppermute x45, waiting for transfers between devices, allsum(): lax.ppermute(value, axis, [(i, i ^ step) for i in range(count)])  153 us
    gather x1, local copies, waits for them, and re-layouts, on_device(): permuted = jnp.take(coarse_rows, positions, axis=1)  57.6 us
    ppermute x16, starting transfers between devices, neighbours(): return (lax.ppermute(rows[1], axis, up), lax.ppermute(rows[0], axis, down))  46.6 us
    ppermute x6, waiting for transfers between devices, _test_ends(): reached = lax.ppermute(reached, axis_name=chip_axis, perm=by_place)  19.7 us
    ppermute x6, starting transfers between devices, _test_ends(): reached = lax.ppermute(reached, axis_name=chip_axis, perm=by_place)  16.4 us
  transfers between devices with their start and end apart: 75, of which 57 were waited for; matrix products, arithmetic and copies ran while one was open for 11% of the time, Pallas kernels for 0%

profile of v1, /device:TPU:32, one launch (start us, length us, event | category | flops | bytes accessed | tf_op | source)
XLA Modules:
  0.0 733.3 jit_solution(8799608200374896432)
XLA Ops:
  22.6 5.1 collective-permute-start.4
  32.0 6.7 collective-permute-start.10
  52.5 6.7 collective-permute-start.7
  61.9 12.1 %collective-permute-start.8 = (f32[128]{0:T(128)S(1)}, f32[128]{0:T(128)S(1)}, u32[]{:S(2)}, u32[]{:S(2)}) collective-permute-start(f32[128]{0:T(128)S(1)} %add.329), channel_id=1, source_target_pairs={{0,256},{8,264},{16,272},{24,280},{32,288},{40,296},{48,304},{56,3... | collective-permute-start | bytes 1544 | tf_op jit(solution)/shard_map/ppermute | solution.py:57
  76.2 103.5 %all_gather.6 = bf16[2048,128]{1,0:T(8,128)(2,1)S(1)} all-gather(bf16[32,128]{1,0:T(8,128)(2,1)S(1)} %fusion.6), channel_id=1, replica_groups=mesh['gx'=64,'gy'=8] {'gx'}, dimensions={0}, use_global_device_ids=true | all-gather | bytes 532480 | tf_op jit(solution)/shard_map/all_gather | solution.py:109
  183.0 57.6 %gather_fusion.1 = bf16[16384,32]{1,0:T(8,128)(2,1)} fusion(bf16[32,16384]{0,1:T(8,128)(2,1)} %bitcast.133, s32[16384]{0:T(1024)S(1)} %broadcast_clamp_fusion), kind=kCustom, calls=%fused_computation.1 | custom fusion | bytes 2162688 | tf_op jit(solution)/shard_map/jit(_take)/gather | solution.py:103
  246.9 6.6 collective-permute-done.14
  277.9 7.1 convolution_add_fusion.1
  297.4 5.9 collective-permute-done.20
  316.4 5.0 collective-permute-done.26
  355.0 8.7 %collective-permute-start.32 = (f32[128]{0:T(128)S(1)}, f32[128]{0:T(128)S(1)}, u32[]{:S(2)}, u32[]{:S(2)}) collective-permute-start(f32[128]{0:T(128)S(1)} %add.369), channel_id=1, source_target_pairs={{0,256},{8,264},{16,272},{24,280},{32,288},{40,296},{48,304},{56,3... | collective-permute-start | bytes 1544 | tf_op jit(solution)/shard_map/ppermute | solution.py:57
  363.7 5.5 collective-permute-done.32
  418.3 8.7 %collective-permute-start.41 = (f32[128]{0:T(128)S(1)}, f32[128]{0:T(128)S(1)}, u32[]{:S(2)}, u32[]{:S(2)}) collective-permute-start(f32[128]{0:T(128)S(1)} %add.378), channel_id=1, source_target_pairs={{0,256},{8,264},{16,272},{24,280},{32,288},{40,296},{48,304},{56,3... | collective-permute-start | bytes 1544 | tf_op jit(solution)/shard_map/ppermute | solution.py:57
  432.6 98.2 %all_gather.7 = bf16[2048,128]{1,0:T(8,128)(2,1)S(1)} all-gather(bf16[32,128]{1,0:T(8,128)(2,1)S(1)} %fusion.7), channel_id=1, replica_groups=mesh['gx'=64,'gy'=8] {'gx'}, dimensions={0}, use_global_device_ids=true | all-gather | bytes 532480 | tf_op jit(solution)/shard_map/all_gather | solution.py:109
  569.8 5.4 collective-permute-done.52
  576.1 7.1 convolution_add_fusion
  589.0 5.8 collective-permute-start.54
  596.7 6.0 collective-permute-done.53
  615.8 5.0 collective-permute-done.59
  628.2 5.0 collective-permute-done.61
  645.0 5.7 collective-permute-start.64
  654.4 9.8 %collective-permute-start.65 = (f32[2,128]{1,0:T(2,128)S(1)}, f32[2,128]{1,0:T(2,128)S(1)}, u32[]{:S(2)}, u32[]{:S(2)}) collective-permute-start(f32[2,128]{1,0:T(2,128)S(1)} %add.390), channel_id=1, source_target_pairs={{0,256},{8,264},{16,272},{24,280},{32,288},{40,296},{48,304},{56,3... | collective-permute-start | bytes 3080 | tf_op jit(solution)/shard_map/ppermute | solution.py:57
  708.3 5.7 collective-permute-start.73
  717.7 9.8 %collective-permute-start.74 = (f32[128]{0:T(128)S(1)}, f32[128]{0:T(128)S(1)}, u32[]{:S(2)}, u32[]{:S(2)}) collective-permute-start(f32[128]{0:T(128)S(1)} %add.400), channel_id=1, source_target_pairs={{0,256},{8,264},{16,272},{24,280},{32,288},{40,296},{48,304},{56,3... | collective-permute-start | bytes 1544 | tf_op jit(solution)/shard_map/ppermute | solution.py:57
  (258 shorter events, 329.1 us)
Async XLA Ops:
  22.6 18.1 %collective-permute-start.4 = (f32[128]{0:T(128)S(1)}, f32[128]{0:T(128)S(1)}, u32[]{:S(2)}, u32[]{:S(2)}) collective-permute-start(f32[128]{0:T(128)S(1)} %add.325), channel_id=1, source_target_pairs={{0,16},{8,24},{16,0},{24,8},{32,48},{40,56},{48,32},{56,40},{64,80... | collective-permute-start | bytes 1544 | tf_op jit(solution)/shard_map/ppermute | solution.py:57
  27.7 216.1 %collective-permute-start.12 = (f32[128,128]{1,0:T(8,128)S(1)}, f32[128,128]{1,0:T(8,128)S(1)}, u32[]{:S(2)}, u32[]{:S(2)}) collective-permute-start(f32[128,128]{1,0:T(8,128)S(1)} %get-tuple-element.20), channel_id=1, source_target_pairs={{1,0},{2,1},{3,2},{4,3},{5,4},{6,5},{7,6},{9,8},{10,9},{11,10},{12... | collective-permute-start | bytes 196616 | tf_op jit(solution)/shard_map/ppermute | solution.py:40
  29.0 217.8 %collective-permute-start.11 = (f32[128,128]{1,0:T(8,128)S(1)}, f32[128,128]{1,0:T(8,128)S(1)}, u32[]{:S(2)}, u32[]{:S(2)}) collective-permute-start(f32[128,128]{1,0:T(8,128)S(1)} %get-tuple-element.18), channel_id=1, source_target_pairs={{0,1},{1,2},{2,3},{3,4},{4,5},{5,6},{6,7},{8,9},{9,10},{10,11},{11... | collective-permute-start | bytes 196616 | tf_op jit(solution)/shard_map/ppermute | solution.py:40
  32.0 214.8 %collective-permute-start.10 = (f32[128,128]{1,0:T(8,128)S(1)}, f32[128,128]{1,0:T(8,128)S(1)}, u32[]{:S(2)}, u32[]{:S(2)}) collective-permute-start(f32[128,128]{1,0:T(8,128)S(1)} %get-tuple-element.19), channel_id=1, source_target_pairs={{8,0},{16,8},{24,16},{32,24},{40,32},{48,40},{56,48},{64,56},{72,6... | collective-permute-start | bytes 196616 | tf_op jit(solution)/shard_map/ppermute | solution.py:40
  38.7 208.1 %collective-permute-start.9 = (f32[128,128]{1,0:T(8,128)S(1)}, f32[128,128]{1,0:T(8,128)S(1)}, u32[]{:S(2)}, u32[]{:S(2)}) collective-permute-start(f32[128,128]{1,0:T(8,128)S(1)} %get-tuple-element.17), channel_id=1, source_target_pairs={{0,8},{8,16},{16,24},{24,32},{32,40},{40,48},{48,56},{56,64},{64,7... | collective-permute-start | bytes 196616 | tf_op jit(solution)/shard_map/ppermute | solution.py:40
  61.9 14.2 %collective-permute-start.8 = (f32[128]{0:T(128)S(1)}, f32[128]{0:T(128)S(1)}, u32[]{:S(2)}, u32[]{:S(2)}) collective-permute-start(f32[128]{0:T(128)S(1)} %add.329), channel_id=1, source_target_pairs={{0,256},{8,264},{16,272},{24,280},{32,288},{40,296},{48,304},{56,3... | collective-permute-start | bytes 1544 | tf_op jit(solution)/shard_map/ppermute | solution.py:57
  179.7 67.1 %collective-permute-start.13 = (bf16[2048,128]{1,0:T(8,128)(2,1)S(1)}, bf16[2048,128]{1,0:T(8,128)(2,1)S(1)}, u32[]{:S(2)}, u32[]{:S(2)}) collective-permute-start(bf16[2048,128]{1,0:T(8,128)(2,1)S(1)} %all_gather.6), channel_id=1, source_target_pairs={{0,1},{1,2},{2,3},{3,4},{4,5},{5,6},{6,7},{7,0},{8,9},{9,10},{10,1... | collective-permute-start | bytes 1572872 | tf_op jit(solution)/shard_map/ppermute | solution.py:26
  246.8 10.0 %collective-permute-start.15 = (bf16[2048,128]{1,0:T(8,128)(2,1)S(1)}, bf16[2048,128]{1,0:T(8,128)(2,1)S(1)}, u32[]{:S(2)}, u32[]{:S(2)}) collective-permute-start(bf16[2048,128]{1,0:T(8,128)(2,1)S(1)} %collective-permute-done.13), channel_id=1, source_target_pairs={{0,1},{1,2},{2,3},{3,4},{4,5},{5,6},{6,7},{7,0},{8,9},{9,10},{10,1... | collective-permute-start | bytes 1572872 | tf_op jit(solution)/shard_map/ppermute | solution.py:26
  253.4 9.8 %collective-permute-start.16 = (bf16[2048,128]{1,0:T(8,128)(2,1)S(1)}, bf16[2048,128]{1,0:T(8,128)(2,1)S(1)}, u32[]{:S(2)}, u32[]{:S(2)}) collective-permute-start(bf16[2048,128]{1,0:T(8,128)(2,1)S(1)} %collective-permute-done.14), channel_id=1, source_target_pairs={{0,7},{1,0},{2,1},{3,2},{4,3},{5,4},{6,5},{7,6},{8,15},{9,8},{10,9... | collective-permute-start | bytes 1572872 | tf_op jit(solution)/shard_map/ppermute | solution.py:29
  256.8 10.4 %collective-permute-start.17 = (bf16[2048,128]{1,0:T(8,128)(2,1)S(1)}, bf16[2048,128]{1,0:T(8,128)(2,1)S(1)}, u32[]{:S(2)}, u32[]{:S(2)}) collective-permute-start(bf16[2048,128]{1,0:T(8,128)(2,1)S(1)} %collective-permute-done.15), channel_id=1, source_target_pairs={{0,1},{1,2},{2,3},{3,4},{4,5},{5,6},{6,7},{7,0},{8,9},{9,10},{10,1... | collective-permute-start | bytes 1572872 | tf_op jit(solution)/shard_map/ppermute | solution.py:26
  267.2 9.8 %collective-permute-start.19 = (bf16[2048,128]{1,0:T(8,128)(2,1)S(1)}, bf16[2048,128]{1,0:T(8,128)(2,1)S(1)}, u32[]{:S(2)}, u32[]{:S(2)}) collective-permute-start(bf16[2048,128]{1,0:T(8,128)(2,1)S(1)} %collective-permute-done.17), channel_id=1, source_target_pairs={{0,1},{1,2},{2,3},{3,4},{4,5},{5,6},{6,7},{7,0},{8,9},{9,10},{10,1... | collective-permute-start | bytes 1572872 | tf_op jit(solution)/shard_map/ppermute | solution.py:26
  286.5 10.9 %collective-permute-start.23 = (bf16[128,128]{1,0:T(8,128)(2,1)S(1)}, bf16[128,128]{1,0:T(8,128)(2,1)S(1)}, u32[]{:S(2)}, u32[]{:S(2)}) collective-permute-start(bf16[128,128]{1,0:T(8,128)(2,1)S(1)} %get-tuple-element.28), channel_id=1, source_target_pairs={{1,0},{2,1},{3,2},{4,3},{5,4},{6,5},{7,6},{9,8},{10,9},{11,10},{12... | collective-permute-start | bytes 98312 | tf_op jit(solution)/shard_map/ppermute | solution.py:40
  355.0 14.2 %collective-permute-start.32 = (f32[128]{0:T(128)S(1)}, f32[128]{0:T(128)S(1)}, u32[]{:S(2)}, u32[]{:S(2)}) collective-permute-start(f32[128]{0:T(128)S(1)} %add.369), channel_id=1, source_target_pairs={{0,256},{8,264},{16,272},{24,280},{32,288},{40,296},{48,304},{56,3... | collective-permute-start | bytes 1544 | tf_op jit(solution)/shard_map/ppermute | solution.py:57
  418.3 14.2 %collective-permute-start.41 = (f32[128]{0:T(128)S(1)}, f32[128]{0:T(128)S(1)}, u32[]{:S(2)}, u32[]{:S(2)}) collective-permute-start(f32[128]{0:T(128)S(1)} %add.378), channel_id=1, source_target_pairs={{0,256},{8,264},{16,272},{24,280},{32,288},{40,296},{48,304},{56,3... | collective-permute-start | bytes 1544 | tf_op jit(solution)/shard_map/ppermute | solution.py:57
  530.8 15.0 %collective-permute-start.46 = (bf16[2048,128]{1,0:T(8,128)(2,1)S(1)}, bf16[2048,128]{1,0:T(8,128)(2,1)S(1)}, u32[]{:S(2)}, u32[]{:S(2)}) collective-permute-start(bf16[2048,128]{1,0:T(8,128)(2,1)S(1)} %all_gather.7), channel_id=1, source_target_pairs={{0,1},{1,2},{2,3},{3,4},{4,5},{5,6},{6,7},{7,0},{8,9},{9,10},{10,1... | collective-permute-start | bytes 1572872 | tf_op jit(solution)/shard_map/ppermute | solution.py:26
  530.8 10.9 %collective-permute-start.45 = (f32[128,128]{1,0:T(8,128)S(1)}, f32[128,128]{1,0:T(8,128)S(1)}, u32[]{:S(2)}, u32[]{:S(2)}) collective-permute-start(f32[128,128]{1,0:T(8,128)S(1)} %get-tuple-element.16), channel_id=1, source_target_pairs={{1,0},{2,1},{3,2},{4,3},{5,4},{6,5},{7,6},{9,8},{10,9},{11,10},{12... | collective-permute-start | bytes 196616 | tf_op jit(solution)/shard_map/ppermute | solution.py:40
  532.1 13.8 %collective-permute-start.44 = (f32[128,128]{1,0:T(8,128)S(1)}, f32[128,128]{1,0:T(8,128)S(1)}, u32[]{:S(2)}, u32[]{:S(2)}) collective-permute-start(f32[128,128]{1,0:T(8,128)S(1)} %get-tuple-element.14), channel_id=1, source_target_pairs={{0,1},{1,2},{2,3},{3,4},{4,5},{5,6},{6,7},{8,9},{9,10},{10,11},{11... | collective-permute-start | bytes 196616 | tf_op jit(solution)/shard_map/ppermute | solution.py:40
  535.2 10.8 %collective-permute-start.43 = (f32[128,128]{1,0:T(8,128)S(1)}, f32[128,128]{1,0:T(8,128)S(1)}, u32[]{:S(2)}, u32[]{:S(2)}) collective-permute-start(f32[128,128]{1,0:T(8,128)S(1)} %get-tuple-element.15), channel_id=1, source_target_pairs={{8,0},{16,8},{24,16},{32,24},{40,32},{48,40},{56,48},{64,56},{72,6... | collective-permute-start | bytes 196616 | tf_op jit(solution)/shard_map/ppermute | solution.py:40
  545.8 9.8 %collective-permute-start.48 = (bf16[2048,128]{1,0:T(8,128)(2,1)S(1)}, bf16[2048,128]{1,0:T(8,128)(2,1)S(1)}, u32[]{:S(2)}, u32[]{:S(2)}) collective-permute-start(bf16[2048,128]{1,0:T(8,128)(2,1)S(1)} %collective-permute-done.46), channel_id=1, source_target_pairs={{0,1},{1,2},{2,3},{3,4},{4,5},{5,6},{6,7},{7,0},{8,9},{9,10},{10,1... | collective-permute-start | bytes 1572872 | tf_op jit(solution)/shard_map/ppermute | solution.py:26
  565.4 9.8 %collective-permute-start.52 = (bf16[2048,128]{1,0:T(8,128)(2,1)S(1)}, bf16[2048,128]{1,0:T(8,128)(2,1)S(1)}, u32[]{:S(2)}, u32[]{:S(2)}) collective-permute-start(bf16[2048,128]{1,0:T(8,128)(2,1)S(1)} %collective-permute-done.50), channel_id=1, source_target_pairs={{0,1},{1,2},{2,3},{3,4},{4,5},{5,6},{6,7},{7,0},{8,9},{9,10},{10,1... | collective-permute-start | bytes 1572872 | tf_op jit(solution)/shard_map/ppermute | solution.py:26
  584.6 12.0 %collective-permute-start.56 = (bf16[128,128]{1,0:T(8,128)(2,1)S(1)}, bf16[128,128]{1,0:T(8,128)(2,1)S(1)}, u32[]{:S(2)}, u32[]{:S(2)}) collective-permute-start(bf16[128,128]{1,0:T(8,128)(2,1)S(1)} %get-tuple-element.24), channel_id=1, source_target_pairs={{1,0},{2,1},{3,2},{4,3},{5,4},{6,5},{7,6},{9,8},{10,9},{11,10},{12... | collective-permute-start | bytes 98312 | tf_op jit(solution)/shard_map/ppermute | solution.py:40
  585.9 10.7 %collective-permute-start.55 = (bf16[128,128]{1,0:T(8,128)(2,1)S(1)}, bf16[128,128]{1,0:T(8,128)(2,1)S(1)}, u32[]{:S(2)}, u32[]{:S(2)}) collective-permute-start(bf16[128,128]{1,0:T(8,128)(2,1)S(1)} %get-tuple-element.22), channel_id=1, source_target_pairs={{0,1},{1,2},{2,3},{3,4},{4,5},{5,6},{6,7},{8,9},{9,10},{10,11},{11... | collective-permute-start | bytes 98312 | tf_op jit(solution)/shard_map/ppermute | solution.py:40
  654.4 14.2 %collective-permute-start.65 = (f32[2,128]{1,0:T(2,128)S(1)}, f32[2,128]{1,0:T(2,128)S(1)}, u32[]{:S(2)}, u32[]{:S(2)}) collective-permute-start(f32[2,128]{1,0:T(2,128)S(1)} %add.390), channel_id=1, source_target_pairs={{0,256},{8,264},{16,272},{24,280},{32,288},{40,296},{48,304},{56,3... | collective-permute-start | bytes 3080 | tf_op jit(solution)/shard_map/ppermute | solution.py:57
  717.7 14.2 %collective-permute-start.74 = (f32[128]{0:T(128)S(1)}, f32[128]{0:T(128)S(1)}, u32[]{:S(2)}, u32[]{:S(2)}) collective-permute-start(f32[128]{0:T(128)S(1)} %add.400), channel_id=1, source_target_pairs={{0,256},{8,264},{16,272},{24,280},{32,288},{40,296},{48,304},{56,3... | collective-permute-start | bytes 1544 | tf_op jit(solution)/shard_map/ppermute | solution.py:57
  (58 other events, 1002.2 us)
